TPU v7x, 512 devices: a whole 4x4x16 slice. The times are simulated.
512 devices in a mesh: rows: 32 (over x, y, core), cols: 16 (over z).
Axes of the slice: x: 4, y: 4, z: 16, core: 2. Of those that a mesh axis runs over, the one named last changes fastest.
Arguments:
- panel_t: float32 [256, 65536], P('cols', 'rows'), as said below
- trailing: float32 [65536, 4096], P('rows', 'cols'), may hold values from -6 to 6
- prev_lower_t: float32 [256, 65536], P('cols', 'rows'), may hold values from -6 to 6
- prev_upper: float32 [256, 4096], P(None, 'cols'), may hold values from -0.375 to 0.375
- leaf_picks: int32 [32, 256], P('rows'), may hold values from 0 to 2047, as said below
- merge_picks: int32 [31, 256], replicated, may hold values from 0 to 511, as said below
Outputs:
- lower_t: float32 [256, 65536], P('cols', 'rows')
- upper_left: float32 [256, 256], replicated
- upper_right: float32 [256, 4096], P(None, 'cols')
- updated: float32 [65536, 4096], P('rows', 'cols')
- gram: float32 [256, 256], P('cols')
Inputs may be any that keep to these rules, and one draw needn't show every extreme that they name: `leaf_picks`: each row lists 256 different row numbers within the 2048 rows of one index of rows. `merge_picks`: each row lists 256 different positions in a stack of two candidate lists. `panel_t`: the rows of the panel at the pivots form a strictly diagonally dominant block.
All inputs are finite; a program needn't handle non-finite values.
Results may differ from a plain program's by a relative error of at most 0.0003.
Values sent between devices are 32-bit elements; how exact they have to be, the bound alone decides.
No kernel may reach another device: no remote copies, remote signals or barrier semaphores. Data moves between devices by JAX's collectives and lax.ppermute only.
A program may use at most 64 MiB of HBM per device.

v0:
```python
import jax
import jax.numpy as jnp
from jax import lax
from jax.sharding import PartitionSpec as P

full_precision = lax.Precision.HIGHEST


def from_partner(shard, axis, apart):
    return lax.ppermute(shard, axis, [(i, i ^ 1 << apart) for i in range(lax.axis_size(axis))])


def trace_pivots(merge_picks, row_devices):
    list_width = merge_picks.shape[1]
    leaf_group = jnp.zeros((list_width,), jnp.int32)
    leaf_slot = jnp.arange(list_width, dtype=jnp.int32)
    levels = row_devices.bit_length() - 1
    for section in reversed(range(levels)):
        offset_rows = row_devices - (row_devices >> section)
        position = merge_picks[offset_rows + leaf_group, leaf_slot]
        right_side = (position >= list_width).astype(jnp.int32)
        leaf_group = 2 * leaf_group + right_side
        leaf_slot = position - list_width * right_side
    return (leaf_group, leaf_slot)


def product(left_side, right_side):
    return jnp.dot(left_side, right_side, precision=full_precision)


def unit_lower_inverse(lower):
    order = lower.shape[0]
    identity = jnp.eye(order, dtype=jnp.float32)
    power = identity - lower
    result = identity + power
    covered = 1
    while covered < order - 1:
        power = product(power, power)
        result = product(result, identity + power)
        covered = 2 * covered + 1
    return result


def upper_inverse(upper):
    diagonal = jnp.diagonal(upper)
    scaled = upper / diagonal[:, None]
    unit_inverse = unit_lower_inverse(scaled.T).T
    return unit_inverse / diagonal[None, :]


def small_factor(matrix):
    order = matrix.shape[0]
    row_index = lax.broadcasted_iota(jnp.int32, (order, order), 0)
    col_index = lax.broadcasted_iota(jnp.int32, (order, order), 1)
    line_index = jnp.arange(order, dtype=jnp.int32)
    reduced = matrix
    for column_index in range(order - 1):
        pivot_line = jnp.sum(jnp.where(row_index == column_index, reduced, 0.0), 0)
        pivot_column = jnp.sum(jnp.where(col_index == column_index, reduced, 0.0), 1)
        pivot_value = jnp.sum(jnp.where(line_index == column_index, pivot_line, 0.0))
        factors = jnp.where(line_index > column_index, pivot_column / pivot_value, 0.0)
        below = row_index > column_index
        reduced = jnp.where(
            below & (col_index > column_index),
            reduced - factors[:, None] * pivot_line[None, :],
            reduced,
        )
        reduced = jnp.where(below & (col_index == column_index), factors[:, None], reduced)
    return (jnp.tril(reduced, -1) + jnp.eye(order, dtype=matrix.dtype), jnp.triu(reduced))


def factor(matrix):
    order = matrix.shape[0]
    if order <= 32:
        return small_factor(matrix)
    middle_index = order // 2
    lower_head, upper_head = factor(matrix[:middle_index, :middle_index])
    upper_side = product(unit_lower_inverse(lower_head), matrix[:middle_index, middle_index:])
    lower_side = product(matrix[middle_index:, :middle_index], upper_inverse(upper_head))
    schur_block = matrix[middle_index:, middle_index:] - product(lower_side, upper_side)
    lower_tail, upper_tail = factor(schur_block)
    zero_upper = jnp.zeros((middle_index, order - middle_index), matrix.dtype)
    zero_lower = jnp.zeros((order - middle_index, middle_index), matrix.dtype)
    lower_full = jnp.concatenate(
        [
            jnp.concatenate([lower_head, zero_upper], 1),
            jnp.concatenate([lower_side, lower_tail], 1),
        ],
        0,
    )
    upper_full = jnp.concatenate(
        [
            jnp.concatenate([upper_head, upper_side], 1),
            jnp.concatenate([zero_lower, upper_tail], 1),
        ],
        0,
    )
    return (lower_full, upper_full)


def contract_first(left_side, right_side):
    return lax.dot_general(
        left_side, right_side, (((0,), (0,)), ((), ())), precision=full_precision
    )


def contract_second(left_side, right_side):
    return lax.dot_general(
        left_side, right_side, (((1,), (1,)), ((), ())), precision=full_precision
    )


def body(panel_t, trailing, prev_lower_t, prev_upper, leaf_picks, merge_picks):
    slab_rows = panel_t.shape[0]
    rows_here = panel_t.shape[1]
    row_devices = lax.axis_size("rows")
    own_row = lax.axis_index("rows")
    own_column = lax.axis_index("cols")
    leaf_group, leaf_slot = trace_pivots(merge_picks, row_devices)
    owner_mask = leaf_group == own_row
    local_rows = jnp.take(leaf_picks[0], leaf_slot)
    middle = trailing
    middle = middle - contract_first(
        lax.all_gather(prev_lower_t, "cols", axis=0, tiled=True), prev_upper
    )
    panel_full = lax.all_gather(panel_t, "cols", axis=0, tiled=True)
    middle, panel_full = (middle, panel_full)
    candidates = jnp.take(panel_t, leaf_picks[0], axis=1)
    levels = row_devices.bit_length() - 1
    for section in range(levels):
        partner = from_partner(candidates, "rows", section)
        upper_half = own_row >> section & 1
        stacked = jnp.where(
            upper_half == 0,
            jnp.concatenate([candidates, partner], 1),
            jnp.concatenate([partner, candidates], 1),
        )
        merge_index = row_devices - (row_devices >> section) + (own_row >> section + 1)
        selection = lax.dynamic_index_in_dim(merge_picks, merge_index, 0, keepdims=False)
        candidates = jnp.take(stacked, selection, axis=1)
    block_t = lax.all_gather(candidates, "cols", axis=0, tiled=True)
    lower_left, upper_left = factor(block_t.T)
    inverse = upper_inverse(upper_left)
    chosen_rows = jnp.take(middle, local_rows, axis=0)
    pivot_trailing = lax.psum(jnp.where(owner_mask[:, None], chosen_rows, 0.0), "rows")
    upper_right = product(unit_lower_inverse(lower_left), pivot_trailing)
    lower_full = jnp.dot(inverse.T, panel_full, precision=full_precision)
    lower_tile = lax.dynamic_slice_in_dim(lower_full, own_column * slab_rows, slab_rows, 0)
    updated = middle - contract_first(lower_full, upper_right)
    gram_rows = contract_second(lower_tile, lower_full)
    gram = lax.psum(gram_rows, "rows") / (rows_here * row_devices)
    return (lower_tile, upper_left, upper_right, updated, gram)


def solution(mesh):
    return jax.shard_map(
        body,
        mesh=mesh,
        in_specs=(
            P("cols", "rows"),
            P("rows", "cols"),
            P("cols", "rows"),
            P(None, "cols"),
            P("rows", None),
            P(),
        ),
        out_specs=(P("cols", "rows"), P(), P(None, "cols"), P("rows", "cols"), P("cols", None)),
        check_vma=False,
    )
```

profile of v0, /device:TPU:1, one launch (start us, length us, event | category | flops | bytes accessed | tf_op | source)
XLA Modules:
  0.0 666.7 jit_solution(18420080270595223450)
XLA Ops:
  9.2 2.5 gather_fusion.9
  11.8 2.3 gather_fusion.10
  14.1 2.3 gather_fusion.11
  16.5 2.3 gather_fusion.12
  18.9 2.3 gather_fusion.13
  22.2 8.8 %collective-permute-start = (f32[16,256]{0,1:T(8,128)S(1)}, f32[16,256]{0,1:T(8,128)S(1)}, u32[]{:S(2)}, u32[]{:S(2)}) collective-permute-start(f32[16,256]{0,1:T(8,128)S(1)} %select_bitcast_fusion.4), channel_id=1, source_target_pairs={{0,16},{16,0},{32,48},{48,32},{64,80},{80,64},{96,112},{112,96},{1... | collective-permute-start | bytes 49160 | tf_op jit(solution)/shard_map/ppermute | solution.py:10
  31.8 1.9 gather_fusion.14
  34.8 1.9 collective-permute-start.1
  36.7 5.1 collective-permute-done.1
  42.6 1.9 collective-permute-start.2
  44.6 5.7 collective-permute-done.2
  51.1 1.9 collective-permute-start.3
  53.1 3.8 collective-permute-done.3
  57.7 1.9 collective-permute-start.4
  60.2 4.8 collective-permute-done.4
  65.8 27.0 %all_gather.9 = f32[256,256]{1,0:T(8,128)S(1)} all-gather(f32[16,256]{1,0:T(8,128)S(1)} %select_bitcast_fusion.5), channel_id=1, replica_groups=mesh['rows'=32,'cols'=16] {'cols'}, dimensions={0}, use_global_device_ids=true | all-gather | bytes 278528 | tf_op jit(solution)/shard_map/all_gather | solution.py:141
  492.5 2.5 gather_fusion.8
  507.7 6.1 convolution_subtract_fusion.1
  515.7 3.5 fusion.224
  519.2 1.7 fusion.232
  520.9 127.3 %psum.15 = f32[16,256]{1,0:T(8,128)S(1)} all-reduce(f32[16,256]{1,0:T(8,128)S(1)} %fusion.232), channel_id=1, replica_groups=mesh['rows'=32,'cols'=16] {'rows'}, use_global_device_ids=true, to_apply=%region_745.747 | all-reduce | flops 4096 | bytes 32768 | tf_op jit(solution)/shard_map/psum | solution.py:151
  648.8 3.2 all-reduce.16.cloned.1.call-done
  652.0 1.3 fusion.231
  653.3 6.6 convolution_subtract_fusion
  (1113 shorter events, 419.9 us)
Async XLA Ops:
  7.2 500.5 %copy-start = (f32[256,256]{1,0:T(8,128)S(1)}, f32[256,256]{1,0:T(8,128)}, u32[]{:S(2)}) copy-start(f32[256,256]{1,0:T(8,128)} %param.11) | copy-start | bytes 786436
  7.2 4.6 copy-start.2
  7.2 500.5 %all-gather.5.cloned.1.call-start = ((), (), s32[]{:S(2)}) async-start(), calls=%async_computation.1 | async-start | bytes 2228224 | tf_op jit(solution)/shard_map/all_gather | solution.py:124
  7.9 507.7 %all-gather.3.cloned.1.call-start = ((), (), s32[]{:S(2)}) async-start(), calls=%async_computation | async-start | bytes 2228224 | tf_op jit(solution)/shard_map/all_gather | solution.py:126
  14.1 7.1 %copy-start.1 = (s32[1,256]{1,0:T(1,128)S(1)}, s32[1,256]{1,0:T(1,128)}, u32[]{:S(2)}) copy-start(s32[1,256]{1,0:T(1,128)} %param.12) | copy-start | bytes 3076
  22.2 11.7 %collective-permute-start = (f32[16,256]{0,1:T(8,128)S(1)}, f32[16,256]{0,1:T(8,128)S(1)}, u32[]{:S(2)}, u32[]{:S(2)}) collective-permute-start(f32[16,256]{0,1:T(8,128)S(1)} %select_bitcast_fusion.4), channel_id=1, source_target_pairs={{0,16},{16,0},{32,48},{48,32},{64,80},{80,64},{96,112},{112,96},{1... | collective-permute-start | bytes 49160 | tf_op jit(solution)/shard_map/ppermute | solution.py:10
  31.0 621.0 %all-reduce.16.cloned.1.call-start = ((), (), s32[]{:S(2)}) async-start(), calls=%async_computation.2 | async-start | bytes 524288 | tf_op jit(solution)/shard_map/psum | solution.py:145
  34.8 7.0 %collective-permute-start.1 = (f32[16,256]{0,1:T(8,128)S(1)}, f32[16,256]{0,1:T(8,128)S(1)}, u32[]{:S(2)}, u32[]{:S(2)}) collective-permute-start(f32[16,256]{0,1:T(8,128)S(1)} %select_bitcast_fusion.3), channel_id=1, source_target_pairs={{0,32},{16,48},{32,0},{48,16},{64,96},{80,112},{96,64},{112,80},{1... | collective-permute-start | bytes 49160 | tf_op jit(solution)/shard_map/ppermute | solution.py:10
  42.6 7.6 %collective-permute-start.2 = (f32[16,256]{0,1:T(8,128)S(1)}, f32[16,256]{0,1:T(8,128)S(1)}, u32[]{:S(2)}, u32[]{:S(2)}) collective-permute-start(f32[16,256]{0,1:T(8,128)S(1)} %select_bitcast_fusion.2), channel_id=1, source_target_pairs={{0,64},{16,80},{32,96},{48,112},{64,0},{80,16},{96,32},{112,48},{1... | collective-permute-start | bytes 49160 | tf_op jit(solution)/shard_map/ppermute | solution.py:10
  51.1 5.7 collective-permute-start.3
  57.7 7.3 %collective-permute-start.4 = (f32[16,256]{0,1:T(8,128)S(1)}, f32[16,256]{0,1:T(8,128)S(1)}, u32[]{:S(2)}, u32[]{:S(2)}) collective-permute-start(f32[16,256]{0,1:T(8,128)S(1)} %select_bitcast_fusion), channel_id=1, source_target_pairs={{0,256},{16,272},{32,288},{48,304},{64,320},{80,336},{96,352},{112... | collective-permute-start | bytes 49160 | tf_op jit(solution)/shard_map/ppermute | solution.py:10
  513.8 1.9 copy-start.3
  519.2 140.8 %copy-start.5 = (f32[16,2048]{1,0:T(8,128)}, f32[16,2048]{1,0:T(8,128)S(1)}, u32[]{:S(2)}) copy-start(f32[16,2048]{1,0:T(8,128)S(1)} %constant_dynamic-slice_fusion) | copy-start | bytes 393220
  653.3 6.6 copy-start.4
Sparse Core Ops, SparseCore 0:
  10.1 69.7 all-gather.4
  81.9 70.5 all-gather.2
  515.7 136.2 all-reduce.15
where the time goes:
time: 674 us; the launch traced here: 667 us
  other arithmetic  362 us (54%)
  blocking collectives  154 us (23%)
  matrix products  59.6 us (9%)
  local copies, waits for them, and re-layouts  33.2 us (5%)
  waiting for transfers between devices  23.2 us (3%)
  between operations  18.1 us (3%)
  starting transfers between devices  16.6 us (2%)
    select_n x248, other arithmetic, small_factor(): jnp.where(line_index > column_index, pivot_column / pivot_value, 0.0)  161 us
    reduce_sum x248, other arithmetic, small_factor(): jnp.sum(jnp.where(line_index == column_index, pivot_line, 0.0))  151 us
    psum x1, blocking collectives, body(): gram = lax.psum(gram_rows, 'rows') / (rows_here * row_devices)  127 us
    reduce_sum x244, other arithmetic, small_factor(): jnp.sum(jnp.where(col_index == column_index, reduced, 0.0), 1)  45.1 us
    dot_general x178, matrix products, product(): return jnp.dot(left_side, right_side, precision=full_precision)  41.6 us
    all_gather x1, blocking collectives, body(): block_t = lax.all_gather(candidates, 'cols', axis=0, tiled=True)  27 us
    ppermute x5, waiting for transfers between devices, from_partner(): lax.ppermute(shard, axis, [(i, i ^ 1 << apart) for i in range(lax.axis_si...  19.3 us
    ppermute x5, starting transfers between devices, from_partner(): lax.ppermute(shard, axis, [(i, i ^ 1 << apart) for i in range(lax.axis_si...  16.5 us
  transfers between devices with their start and end apart: 8, of which 5 were waited for; matrix products, arithmetic and copies ran while one was open for 67% of the time, Pallas kernels for 0%

commit v1 on v0

--- a/solution.py
+++ b/solution.py
@@ -4,6 +4,27 @@
 from jax.sharding import PartitionSpec as P
 
 full_precision = lax.Precision.HIGHEST
+
+
+def ring_gather(x, axis, dim):
+    count, here, extent = (lax.axis_size(axis), lax.axis_index(axis), x.shape[dim])
+    upward = [(i, (i + 1) % count) for i in range(count)]
+    left = [(i, (i - 1) % count) for i in range(count)]
+    out = jnp.zeros((*x.shape[:dim], count * extent, *x.shape[dim + 1 :]), x.dtype)
+    out = lax.dynamic_update_slice_in_dim(out, x, here * extent, axis=dim)
+    from_left = from_right = x
+    halfway = count // 2
+    for lap in range(1, halfway + 1):
+        from_left = lax.ppermute(from_left, axis, upward)
+        out = lax.dynamic_update_slice_in_dim(
+            out, from_left, (here - lap) % count * extent, axis=dim
+        )
+        if lap < count - halfway:
+            from_right = lax.ppermute(from_right, axis, left)
+            out = lax.dynamic_update_slice_in_dim(
+                out, from_right, (here + lap) % count * extent, axis=dim
+            )
+    return out
 
 
 def from_partner(shard, axis, apart):
@@ -138,7 +159,7 @@
         merge_index = row_devices - (row_devices >> section) + (own_row >> section + 1)
         selection = lax.dynamic_index_in_dim(merge_picks, merge_index, 0, keepdims=False)
         candidates = jnp.take(stacked, selection, axis=1)
-    block_t = lax.all_gather(candidates, "cols", axis=0, tiled=True)
+    block_t = ring_gather(candidates, "cols", 0)
     lower_left, upper_left = factor(block_t.T)
     inverse = upper_inverse(upper_left)
     chosen_rows = jnp.take(middle, local_rows, axis=0)

time: 674 us -> 711 us (1.055)
  starting transfers between devices: 16.6 us -> 65.9 us
  blocking collectives: 154 us -> 126 us
  waiting for transfers between devices: 23.2 us -> 33.4 us
    ppermute x0 -> x15, starting transfers between devices: none -> 49.3 us  [the longest x7 33.8 us: ring_gather(): from_right = lax.ppermute(from_right, axis, left)]
    all_gather x1 -> x0, blocking collectives: 27 us -> none  [body(): block_t = lax.all_gather(candidates, 'cols', axis=0, tiled=True)]
  transfers between devices with their start and end apart: 8 -> 23, of which waited for: 5 -> 6; matrix products, arithmetic and copies ran while one was open for 67% -> 63% of each run, Pallas kernels for 0% -> 0%
where the time goes in v1:
time: 711 us; the launch traced here: 702 us
  other arithmetic  362 us (51%)
  blocking collectives  126 us (18%)
  starting transfers between devices  65.9 us (9%)
  matrix products  60.1 us (8%)
  local copies, waits for them, and re-layouts  35 us (5%)
  waiting for transfers between devices  33.4 us (5%)
  between operations  19.3 us (3%)
    select_n x248, other arithmetic, small_factor(): jnp.where(line_index > column_index, pivot_column / pivot_value, 0.0)  161 us
    reduce_sum x248, other arithmetic, small_factor(): jnp.sum(jnp.where(line_index == column_index, pivot_line, 0.0))  151 us
    psum x1, blocking collectives, body(): gram = lax.psum(gram_rows, 'rows') / (rows_here * row_devices)  126 us
    reduce_sum x244, other arithmetic, small_factor(): jnp.sum(jnp.where(col_index == column_index, reduced, 0.0), 1)  45.1 us
    dot_general x178, matrix products, product(): return jnp.dot(left_side, right_side, precision=full_precision)  41.2 us
    ppermute x7, starting transfers between devices, ring_gather(): from_right = lax.ppermute(from_right, axis, left)  33.8 us
    ppermute x5, waiting for transfers between devices, from_partner(): lax.ppermute(shard, axis, [(i, i ^ 1 << apart) for i in range(lax.axis_si...  19.8 us
    ppermute x5, starting transfers between devices, from_partner(): lax.ppermute(shard, axis, [(i, i ^ 1 << apart) for i in range(lax.axis_si...  16.5 us
  transfers between devices with their start and end apart: 23, of which 6 were waited for; matrix products, arithmetic and copies ran while one was open for 63% of the time, Pallas kernels for 0%

profile of v1, /device:TPU:1, one launch (start us, length us, event | category | flops | bytes accessed | tf_op | source)
XLA Modules:
  0.0 701.9 jit_solution(1022512508567579775)
XLA Ops:
  9.2 2.5 gather_fusion.9
  11.8 2.3 gather_fusion.10
  14.1 2.3 gather_fusion.11
  16.5 2.3 gather_fusion.12
  22.2 8.8 %collective-permute-start = (f32[16,256]{0,1:T(8,128)S(1)}, f32[16,256]{0,1:T(8,128)S(1)}, u32[]{:S(2)}, u32[]{:S(2)}) collective-permute-start(f32[16,256]{0,1:T(8,128)S(1)} %select_bitcast_fusion.4), channel_id=1, source_target_pairs={{0,16},{16,0},{32,48},{48,32},{64,80},{80,64},{96,112},{112,96},{1... | collective-permute-start | bytes 49160 | tf_op jit(solution)/shard_map/ppermute | solution.py:31
  36.7 5.1 collective-permute-done.1
  44.6 5.7 collective-permute-done.2
  53.1 3.8 collective-permute-done.3
  59.7 5.3 collective-permute-done.4
  67.8 6.3 collective-permute-start.6
  76.9 4.6 collective-permute-start.8
  83.5 4.6 collective-permute-start.10
  90.0 4.6 collective-permute-start.12
  96.6 4.6 collective-permute-start.14
  103.1 4.6 collective-permute-start.16
  109.7 4.6 collective-permute-start.18
  116.5 4.1 collective-permute-done.19
  520.4 2.6 gather_fusion.8
  535.6 3.7 fusion.224
  539.4 7.0 convolution_subtract_fusion.1
  546.4 2.6 gather_fusion.15
  551.5 126.3 %psum.15 = f32[16,256]{1,0:T(8,128)S(1)} all-reduce(f32[16,256]{1,0:T(8,128)S(1)} %fusion.232), channel_id=1, replica_groups=mesh['rows'=32,'cols'=16] {'rows'}, use_global_device_ids=true, to_apply=%region_745.747 | all-reduce | flops 4096 | bytes 32768 | tf_op jit(solution)/shard_map/psum | solution.py:172
  678.4 8.7 %all-reduce.16.cloned.1.call-done = f32[256,256]{1,0:T(8,128)} async-done(((f32[256,256]{1,0:T(8,128)}), f32[256,256]{1,0:T(8,128)}) %all-reduce.16.cloned.1.call-update) | async-done | bytes 262160 | tf_op jit(solution)/shard_map/psum | solution.py:166
  688.5 6.5 convolution_subtract_fusion
  (1156 shorter events, 449.3 us)
Async XLA Ops:
  7.2 532.2 %copy-start = (f32[256,256]{1,0:T(8,128)S(1)}, f32[256,256]{1,0:T(8,128)}, u32[]{:S(2)}) copy-start(f32[256,256]{1,0:T(8,128)} %param.11) | copy-start | bytes 786436
  7.2 528.4 %all-gather.3.cloned.1.call-start = ((), (), s32[]{:S(2)}) async-start(), calls=%async_computation | async-start | bytes 2228224 | tf_op jit(solution)/shard_map/all_gather | solution.py:147
  7.9 531.4 %all-gather.5.cloned.1.call-start = ((), (), s32[]{:S(2)}) async-start(), calls=%async_computation.1 | async-start | bytes 2228224 | tf_op jit(solution)/shard_map/all_gather | solution.py:145
  22.2 11.7 %collective-permute-start = (f32[16,256]{0,1:T(8,128)S(1)}, f32[16,256]{0,1:T(8,128)S(1)}, u32[]{:S(2)}, u32[]{:S(2)}) collective-permute-start(f32[16,256]{0,1:T(8,128)S(1)} %select_bitcast_fusion.4), channel_id=1, source_target_pairs={{0,16},{16,0},{32,48},{48,32},{64,80},{80,64},{96,112},{112,96},{1... | collective-permute-start | bytes 49160 | tf_op jit(solution)/shard_map/ppermute | solution.py:31
  31.0 656.2 %all-reduce.16.cloned.1.call-start = ((), (), s32[]{:S(2)}) async-start(), calls=%async_computation.2 | async-start | bytes 524288 | tf_op jit(solution)/shard_map/psum | solution.py:166
  34.8 7.0 collective-permute-start.1
  42.6 7.6 %collective-permute-start.2 = (f32[16,256]{0,1:T(8,128)S(1)}, f32[16,256]{0,1:T(8,128)S(1)}, u32[]{:S(2)}, u32[]{:S(2)}) collective-permute-start(f32[16,256]{0,1:T(8,128)S(1)} %select_bitcast_fusion.2), channel_id=1, source_target_pairs={{0,64},{16,80},{32,96},{48,112},{64,0},{80,16},{96,32},{112,48},{1... | collective-permute-start | bytes 49160 | tf_op jit(solution)/shard_map/ppermute | solution.py:31
  51.1 5.7 collective-permute-start.3
  57.7 7.3 %collective-permute-start.4 = (f32[16,256]{0,1:T(8,128)S(1)}, f32[16,256]{0,1:T(8,128)S(1)}, u32[]{:S(2)}, u32[]{:S(2)}) collective-permute-start(f32[16,256]{0,1:T(8,128)S(1)} %select_bitcast_fusion), channel_id=1, source_target_pairs={{0,256},{16,272},{32,288},{48,304},{64,320},{80,336},{96,352},{112... | collective-permute-start | bytes 49160 | tf_op jit(solution)/shard_map/ppermute | solution.py:31
  65.8 9.1 %collective-permute-start.5 = (f32[16,256]{1,0:T(8,128)S(1)}, f32[16,256]{1,0:T(8,128)S(1)}, u32[]{:S(2)}, u32[]{:S(2)}) collective-permute-start(f32[16,256]{1,0:T(8,128)S(1)} %get-tuple-element.764), channel_id=1, source_target_pairs={{0,1},{1,2},{2,3},{3,4},{4,5},{5,6},{6,7},{7,8},{8,9},{9,10},{10,1... | collective-permute-start | bytes 49160 | tf_op jit(solution)/shard_map/ppermute | solution.py:18
  67.8 9.1 %collective-permute-start.6 = (f32[16,256]{1,0:T(8,128)S(1)}, f32[16,256]{1,0:T(8,128)S(1)}, u32[]{:S(2)}, u32[]{:S(2)}) collective-permute-start(f32[16,256]{1,0:T(8,128)S(1)} %get-tuple-element.764), channel_id=1, source_target_pairs={{0,15},{1,0},{2,1},{3,2},{4,3},{5,4},{6,5},{7,6},{8,7},{9,8},{10,9... | collective-permute-start | bytes 49160 | tf_op jit(solution)/shard_map/ppermute | solution.py:23
  75.0 6.6 collective-permute-start.7
  76.9 6.6 collective-permute-start.8
  81.5 6.6 collective-permute-start.9
  83.5 6.6 collective-permute-start.10
  88.1 6.6 collective-permute-start.11
  90.0 6.6 collective-permute-start.12
  94.6 6.6 collective-permute-start.13
  96.6 6.6 collective-permute-start.14
  101.2 6.6 collective-permute-start.15
  103.1 6.6 collective-permute-start.16
  107.8 6.6 collective-permute-start.17
  109.7 6.8 collective-permute-start.18
  114.3 6.2 collective-permute-start.19
  (4 other events, 28.7 us)
Sparse Core Ops, SparseCore 0:
  10.1 69.2 all-gather.2
  81.5 70.5 all-gather.4
  549.9 137.1 all-reduce.15
